TPU v7x, 256 devices: a whole 4x4x8 slice. The times are simulated.
256 devices in a mesh: feat: 32 (over y, x, core), samp: 8 (over z).
Axes of the slice: x: 4, y: 4, z: 8, core: 2. Of those that a mesh axis runs over, the one named last changes fastest.
Arguments:
- hash_codes: int32 [32, 6144, 1024], P('feat', 'samp'), may hold values from 0 to 4095
- sample_index: int32 [32, 65536], P('feat', 'samp'), may hold values from 0 to 767, as said below
- labels: int32 [8192, 8], P('feat', 'samp'), may hold values 0 or 1
- encoder_first: bfloat16 [32, 1024, 2048], P('feat'), may hold values from -0.1875 to 0.1875
- encoder_second: bfloat16 [32, 2048, 256], P('feat'), may hold values from -0.125 to 0.125
- top_weight: bfloat16 [1024, 1024], replicated, may hold values from -0.1875 to 0.1875
- score_vector: bfloat16 [1024], replicated, may hold values from -0.1875 to 0.1875
Outputs:
- row_grads: float32 [32, 6144, 256], P('feat', 'samp')
- grad_first: float32 [32, 1024, 2048], P('feat', 'samp')
- grad_second: float32 [32, 2048, 256], P('feat', 'samp')
Inputs may be any that keep to these rules, and one draw needn't show every extreme that they name: `sample_index`: for each feature and sample group the slots used by the group's 8192 samples are 0 to some count minus 1, each at least once; for some feature and group that count is 768.
All inputs are finite; a program needn't handle non-finite values. No bound on the sum of `labels` on one device may be relied on, other than what follows from the above.
Results may differ from a plain program's by a relative error of at most 0.019.
Values may be sent and summed in bfloat16 or wider, within the bound.
No kernel may reach another device: no remote copies, remote signals or barrier semaphores. Data moves between devices by JAX's collectives and lax.ppermute only.
A program may use at most 128 MiB of HBM per device.

v0:
```python
import jax
import jax.numpy as jnp
from jax import lax
from jax.sharding import PartitionSpec as P

BUCKETS = 4096
loss_scale = 256.0


def silu_slope(inputs):
    logistic = jax.nn.sigmoid(inputs)
    return logistic * (1.0 + inputs * (1.0 - logistic))


def top_tower(picked, label_block, top_weight, score_vector):
    feats, count, width = picked.shape
    pair_dots = (
        jnp.einsum("fne,hne->nfh", picked, picked, preferred_element_type=jnp.float32)
        * width ** (-0.5)
    ).astype(jnp.bfloat16)
    pair_flat = pair_dots.reshape(count, feats * feats)
    top_pre = jnp.dot(pair_flat, top_weight, preferred_element_type=jnp.float32)
    top_hidden = jax.nn.silu(top_pre).astype(jnp.bfloat16)
    logits = jnp.dot(top_hidden, score_vector, preferred_element_type=jnp.float32)
    dlogit = loss_scale * (jax.nn.sigmoid(logits) - label_block.astype(jnp.float32))
    top_delta = (
        dlogit[:, None] * score_vector.astype(jnp.float32)[None, :] * silu_slope(top_pre)
    ).astype(jnp.bfloat16)
    pair_delta = jnp.einsum(
        "nk,jk->nj", top_delta, top_weight, preferred_element_type=jnp.float32
    ).reshape(count, feats, feats)
    pair_sym = (pair_delta + jnp.swapaxes(pair_delta, 1, 2)).astype(jnp.bfloat16)
    emb_delta = jnp.einsum(
        "nfh,hne->fne", pair_sym, picked, preferred_element_type=jnp.float32
    ) * width ** (-0.5)
    return emb_delta.astype(jnp.bfloat16)


def local(
    hash_codes, sample_index, labels, encoder_first, encoder_second, top_weight, score_vector
):
    feat_count = lax.axis_size("feat")
    encoded = (hash_codes[0].astype(jnp.float32) * (2.0 / (BUCKETS - 1)) - 1.0).astype(jnp.bfloat16)
    first_pre = jnp.dot(encoded, encoder_first[0], preferred_element_type=jnp.float32)
    first_hidden = jax.nn.silu(first_pre).astype(jnp.bfloat16)
    row_table = jnp.dot(first_hidden, encoder_second[0], preferred_element_type=jnp.float32).astype(
        jnp.bfloat16
    )
    positions = sample_index[0]
    slot_count = row_table.shape[0]
    emb_width = row_table.shape[1]
    chosen_rows = jnp.take(row_table, positions, axis=0).reshape(feat_count, -1, emb_width)
    picked = lax.all_to_all(chosen_rows, "feat", split_axis=0, concat_axis=0, tiled=True)
    emb_delta = top_tower(picked, labels[:, 0], top_weight, score_vector)
    returned = lax.all_to_all(emb_delta, "feat", split_axis=0, concat_axis=0, tiled=True)
    row_grads = jax.ops.segment_sum(
        returned.reshape(-1, emb_width).astype(jnp.float32), positions, num_segments=slot_count
    )
    row_delta = row_grads.astype(jnp.bfloat16)
    second_local = jnp.einsum(
        "rk,re->ke", first_hidden, row_delta, preferred_element_type=jnp.float32
    )
    first_back = jnp.einsum(
        "re,ke->rk", row_delta, encoder_second[0], preferred_element_type=jnp.float32
    )
    first_delta = (first_back * silu_slope(first_pre)).astype(jnp.bfloat16)
    first_local = jnp.einsum("rh,rk->hk", encoded, first_delta, preferred_element_type=jnp.float32)
    total_first, total_second = (
        lax.psum(first_local.astype(jnp.bfloat16), "samp").astype(jnp.float32),
        lax.psum(second_local.astype(jnp.bfloat16), "samp").astype(jnp.float32),
    )
    shard_id = lax.axis_index("samp")
    group_count = lax.axis_size("samp")
    first_rows = total_first.shape[0] // group_count
    second_rows = total_second.shape[0] // group_count
    share_first = lax.dynamic_slice_in_dim(total_first, shard_id * first_rows, first_rows, 0)
    share_second = lax.dynamic_slice_in_dim(total_second, shard_id * second_rows, second_rows, 0)
    return (row_grads[None], share_first[None], share_second[None])


def solution(mesh):
    return jax.shard_map(
        local,
        mesh=mesh,
        in_specs=(
            P("feat", "samp", None),
            P("feat", "samp"),
            P("feat", "samp"),
            P("feat", None, None),
            P("feat", None, None),
            P(),
            P(),
        ),
        out_specs=(P("feat", "samp", None), P("feat", "samp", None), P("feat", "samp", None)),
        check_vma=False,
    )
```

profile of v0, /device:TPU:1, one launch (start us, length us, event | category | flops | bytes accessed | tf_op | source)
XLA Modules:
  0.0 400.1 jit_solution(6173155816172626765)
XLA Ops:
  7.2 0.0 copy-start
  7.2 0.9 compare_select_fusion
  8.1 0.5 broadcast.66
  8.7 1.5 reduce.3
  10.2 0.0 copy-start.5
  10.2 9.8 %multiply_convert_fusion.2 = (bf16[768,2048]{1,0:T(8,128)(2,1)S(1)}, f32[768,2048]{1,0:T(8,128)}) fusion(bf16[1,1024,2048]{2,1,0:T(8,128)(2,1)} %param.10, s32[1,768,1024]{2,1,0:T(8,128)} %param.7), kind=kOutput, calls=%fused_computation.6 | convolution fusion | flops 3232235520 | bytes 16777216 | tf_op jit(solution)/shard_map/dot_general | solution.py:44
  20.0 0.0 copy-start.6
  20.0 1.6 copy-done.6
  21.7 0.0 copy-done.5
  21.7 1.0 convolution_convert_fusion.2
  22.7 33.1 %gather_fusion = bf16[8192,256]{1,0:T(8,128)(2,1)} fusion(bf16[768,256]{1,0:T(8,128)(2,1)S(1)} %convolution_convert_fusion.2, s32[8192]{0:T(1024)S(1)} %broadcast_clamp_fusion), kind=kCustom, calls=%fused_computation | custom fusion | bytes 8421376 | tf_op jit(solution)/shard_map/jit(_take)/gather | solution.py:52
  55.7 5.2 %broadcast_select_fusion = bf16[32,256,256]{2,1,0:T(8,128)(2,1)} fusion(bf16[32,256,256]{2,1,0:T(8,128)(2,1)} %bitcast.47, pred[32,256]{1,0:T(8,128)(4,1)S(1)} %compare_and_fusion), kind=kLoop, calls=%fused_computation.11 | loop fusion | flops 2097152 | bytes 8396800 | tf_op jit(solution)/shard_map/jit(_take)/select_n | solution.py:52
  61.0 0.0 copy-start.3
  61.0 0.0 copy-start.4
  61.0 8.8 %all-to-all-start = ((bf16[32,256,256]{2,1,0:T(8,128)(2,1)}), bf16[32,256,256]{2,1,0:T(8,128)(2,1)}, u32[]{:S(2)}, u32[]{:S(2)}) async-start(bf16[32,256,256]{2,1,0:T(8,128)(2,1)} %broadcast_select_fusion), calls=%async_computation | async-start | bytes 8388608 | tf_op jit(solution)/shard_map/all_to_all | solution.py:53
  69.8 0.0 all-reduce.3.cloned.1.call-start
  69.8 0.0 copy-done.3
  69.9 0.0 copy-done.4
  69.9 50.2 %all-to-all-done = bf16[32,256,256]{2,1,0:T(8,128)(2,1)} async-done(((bf16[32,256,256]{2,1,0:T(8,128)(2,1)}), bf16[32,256,256]{2,1,0:T(8,128)(2,1)}, u32[]{:S(2)}, u32[]{:S(2)}) %all-to-all-start) | async-done | bytes 4194336 | tf_op jit(solution)/shard_map/all_to_all | solution.py:53
  120.0 10.2 %fusion.5 = f32[256,32,32]{2,1,0:T(8,128)} fusion(bf16[32,256,256]{2,1,0:T(8,128)(2,1)} %all-to-all-done), kind=kOutput, calls=%fused_computation.13 | convolution fusion | flops 134217728 | bytes 5242880 | tf_op jit(solution)/shard_map/fne,hne->nfh/dot_general | solution.py:18
  130.2 3.5 copy.33
  133.8 0.1 multiply_convert_fusion.5
  133.9 0.0 copy-done
  133.9 0.7 fusion.35
  134.6 0.4 fusion.20
  135.0 1.0 fusion.16
  136.0 0.6 fusion.12
  136.6 3.0 copy.37
  139.7 4.9 %fusion.2 = bf16[32,256,256]{2,0,1:T(8,128)(2,1)S(1)} fusion(bf16[256,32,32]{2,1,0:T(8,128)(2,1)S(1)} %copy.37, bf16[32,256,256]{2,1,0:T(8,128)(2,1)} %all-to-all-done), kind=kOutput, calls=%fused_computation.8 | convolution fusion | flops 138412032 | bytes 8912896 | tf_op jit(solution)/shard_map/nfh,hne->fne/dot_general | solution.py:33
  144.6 2.4 copy.38
  147.0 57.9 %all_to_all.10 = bf16[32,256,256]{2,1,0:T(8,128)(2,1)} all-to-all(bf16[32,256,256]{2,1,0:T(8,128)(2,1)S(1)} %copy.38), channel_id=1, replica_groups=mesh['feat'=32,'samp'=8] {'feat'}, dimensions={0} | all-to-all | bytes 8388608 | tf_op jit(solution)/shard_map/all_to_all | solution.py:55
  204.9 40.9 %scatter_custom_fusion = f32[768,256]{1,0:T(8,128)S(1)} fusion(s32[8192]{0:T(1024)} %bitcast.51, bf16[8192,256]{1,0:T(8,128)(2,1)} %bitcast.46, f32[]{:T(128)} %constant.15.clone.1), kind=kCustom, calls=%fused_computation.2 | custom fusion | flops 4194304 | bytes 4981248 | tf_op jit(solution)/shard_map/scatter-add | solution.py:56
  245.9 0.0 copy-start.2
  245.9 4.2 %convolution_convert_fusion.1 = bf16[2048,256]{1,0:T(8,128)(2,1)} fusion(bf16[768,2048]{1,0:T(8,128)(2,1)} %copy-done.6, f32[768,256]{1,0:T(8,128)S(1)} %scatter_custom_fusion), kind=kOutput, calls=%fused_computation.18 | convolution fusion | flops 806027264 | bytes 4980736 | tf_op jit(solution)/shard_map/rk,re->ke/dot_general | solution.py:60
  250.1 0.0 copy-done.2
  250.1 0.0 copy-start.1
  250.1 10.4 %convolution_convert_fusion = bf16[1024,2048]{1,0:T(8,128)(2,1)} fusion(f32[768,2048]{1,0:T(8,128)} %get-tuple-element.6, bf16[1,2048,256]{2,1,0:T(8,128)(2,1)} %param.11, s32[1,768,1024]{2,1,0:T(8,128)} %param.7, f32[768,256]{1,0:T(8,128)S(1)} %scatter_custom_fusion), kind=kOutput, calls=%fused_computation.12 | convolution fusion | flops 4046127104 | bytes 15466496 | tf_op jit(solution)/shard_map/rh,rk->hk/dot_general | solution.py:67
  260.5 0.0 all-reduce.3.cloned.1.call-update
  260.5 129.0 %all-reduce.3.cloned.1.call-done = (bf16[1024,2048]{1,0:T(8,128)(2,1)}, bf16[2048,256]{1,0:T(8,128)(2,1)}) async-done(((bf16[1024,2048]{1,0:T(8,128)(2,1)}, bf16[2048,256]{1,0:T(8,128)(2,1)}), (bf16[1024,2048]{1,0:T(8,128)(2,1)}, bf16[2048,256]{1,0:T(8,128)(2,1)})) %all-reduce.3.cloned.1.call-update) | async-done | bytes 5242896 | tf_op jit(solution)/shard_map/psum | solution.py:69
  389.5 2.1 convert_bitcast_fusion
  391.6 1.6 convert_bitcast_fusion.1
  393.2 0.0 copy-done.1
  (7 shorter events, 0.1 us)
Async XLA Ops:
  7.2 126.7 %copy-start = (bf16[1024,1024]{1,0:T(8,128)(2,1)S(1)}, bf16[1024,1024]{1,0:T(8,128)(2,1)}, u32[]{:S(2)}) copy-start(bf16[1024,1024]{1,0:T(8,128)(2,1)} %param.12) | copy-start | bytes 6291460
  10.2 11.5 %copy-start.5 = (bf16[1,2048,256]{2,1,0:T(8,128)(2,1)S(1)}, bf16[1,2048,256]{2,1,0:T(8,128)(2,1)}, u32[]{:S(2)}) copy-start(bf16[1,2048,256]{2,1,0:T(8,128)(2,1)} %param.11) | copy-start | bytes 3145732
  20.0 1.6 copy-start.6
  61.0 8.8 %copy-start.3 = (bf16[1024]{0:T(1024)(128)(2,1)S(1)}, bf16[1024]{0:T(1024)(128)(2,1)}, u32[]{:S(2)}) copy-start(bf16[1024]{0:T(1024)(128)(2,1)} %param.13) | copy-start | bytes 6148
  61.0 8.9 %copy-start.4 = (s32[256,1]{0,1:T(1,128)S(1)}, s32[256,1]{0,1:T(1,128)}, u32[]{:S(2)}) copy-start(s32[256,1]{0,1:T(1,128)} %param.9) | copy-start | bytes 3076
  61.0 59.0 %all-to-all-start = ((bf16[32,256,256]{2,1,0:T(8,128)(2,1)}), bf16[32,256,256]{2,1,0:T(8,128)(2,1)}, u32[]{:S(2)}, u32[]{:S(2)}) async-start(bf16[32,256,256]{2,1,0:T(8,128)(2,1)} %broadcast_select_fusion), calls=%async_computation | async-start | bytes 8388608 | tf_op jit(solution)/shard_map/all_to_all | solution.py:53
  69.8 319.7 %all-reduce.3.cloned.1.call-start = ((), (), s32[]{:S(2)}) async-start(), calls=%async_computation.2 | async-start | bytes 10485760 | tf_op jit(solution)/shard_map/psum | solution.py:69
  245.9 4.2 %copy-start.2 = (f32[768,256]{1,0:T(8,128)}, f32[768,256]{1,0:T(8,128)S(1)}, u32[]{:S(2)}) copy-start(f32[768,256]{1,0:T(8,128)S(1)} %scatter_custom_fusion) | copy-start | bytes 2359300
  250.1 143.2 %copy-start.1 = (bf16[1024,1024]{1,0:T(8,128)(2,1)S(1)}, bf16[1024,1024]{1,0:T(8,128)(2,1)}, u32[]{:S(2)}) copy-start(bf16[1024,1024]{1,0:T(8,128)(2,1)} %param.12) | copy-start | bytes 6291460
Sparse Core Ops, SparseCore 0:
  260.6 128.8 all-reduce.2
where the time goes:
time: 401 us; the launch traced here: 400 us
  waiting for transfers between devices  179 us (45%)
  blocking collectives  57.9 us (14%)
  other arithmetic  53.1 us (13%)
  local copies, waits for them, and re-layouts  44.2 us (11%)
  matrix products  42.7 us (11%)
  between operations  14.2 us (4%)
  starting transfers between devices  8.82 us (2%)
    psum x1, waiting for transfers between devices, local(): lax.psum(first_local.astype(jnp.bfloat16), 'samp').astype(jnp.float32)  129 us
    all_to_all x1, blocking collectives, local(): lax.all_to_all(emb_delta, 'feat', split_axis=0, concat_axis=0, tiled=True)  57.9 us
    all_to_all x1, waiting for transfers between devices, local(): lax.all_to_all(chosen_rows, 'feat', split_axis=0, concat_axis=0, tiled=True)  50.2 us
    scatter-add x1, other arithmetic, local(): jax.ops.segment_sum(returned.reshape(-1, emb_width).astype(jnp.float32),...  40.9 us
    gather x1, local copies, waits for them, and re-layouts, local(): jnp.take(row_table, positions, axis=0).reshape(feat_count, -1, emb_width)  33.1 us
    dot_general x1, matrix products, local(): jnp.einsum('rh,rk->hk', encoded, first_delta, preferred_element_type=jnp....  10.4 us
    dot_general x1, matrix products, top_tower(): jnp.einsum('fne,hne->nfh', picked, picked, preferred_element_type=jnp.flo...  10.2 us
    dot_general x1, matrix products, local(): jnp.dot(encoded, encoder_first[0], preferred_element_type=jnp.float32)  9.85 us
  transfers between devices with their start and end apart: 2, of which 2 were waited for; matrix products, arithmetic and copies ran while one was open for 0% of the time, Pallas kernels for 0%

commit v1 on v0

--- a/solution.py
+++ b/solution.py
@@ -5,6 +5,12 @@
 
 BUCKETS = 4096
 loss_scale = 256.0
+
+
+def summed_here(value, axis):
+    parts = lax.all_gather(value, axis, axis=0, tiled=False)
+    result = parts.sum(axis=0)
+    return result
 
 
 def silu_slope(inputs):
@@ -66,7 +72,7 @@
     first_delta = (first_back * silu_slope(first_pre)).astype(jnp.bfloat16)
     first_local = jnp.einsum("rh,rk->hk", encoded, first_delta, preferred_element_type=jnp.float32)
     total_first, total_second = (
-        lax.psum(first_local.astype(jnp.bfloat16), "samp").astype(jnp.float32),
+        summed_here(first_local.astype(jnp.bfloat16), "samp").astype(jnp.float32),
         lax.psum(second_local.astype(jnp.bfloat16), "samp").astype(jnp.float32),
     )
     shard_id = lax.axis_index("samp")

time: 401 us -> 680 us (1.70)
  waiting for transfers between devices: 179 us -> 444 us
  other arithmetic: 53.1 us -> 67.4 us
    all_gather x0 -> x1, waiting for transfers between devices: none -> 333 us  [summed_here(): parts = lax.all_gather(value, axis, axis=0, tiled=False)]
    psum x1, waiting for transfers between devices: 129 us -> 61.5 us  [local(): lax.psum(second_local.astype(jnp.bfloat16), 'samp').astype(jnp.float32)]
    reduce_sum x0 -> x1, other arithmetic: none -> 14.3 us  [summed_here(): result = parts.sum(axis=0)]
  transfers between devices with their start and end apart: 2 -> 3, of which waited for: 2 -> 3; matrix products, arithmetic and copies ran while one was open for 0% -> 2% of each run, Pallas kernels for 0% -> 0%
where the time goes in v1:
time: 680 us; the launch traced here: 679 us
  waiting for transfers between devices  444 us (65%)
  other arithmetic  67.4 us (10%)
  blocking collectives  57.9 us (9%)
  local copies, waits for them, and re-layouts  44.1 us (6%)
  matrix products  42.4 us (6%)
  between operations  14.2 us (2%)
  starting transfers between devices  8.86 us (1%)
    all_gather x1, waiting for transfers between devices, summed_here(): parts = lax.all_gather(value, axis, axis=0, tiled=False)  333 us
    psum x1, waiting for transfers between devices, local(): lax.psum(second_local.astype(jnp.bfloat16), 'samp').astype(jnp.float32)  61.5 us
    all_to_all x1, blocking collectives, local(): lax.all_to_all(emb_delta, 'feat', split_axis=0, concat_axis=0, tiled=True)  57.9 us
    all_to_all x1, waiting for transfers between devices, local(): lax.all_to_all(chosen_rows, 'feat', split_axis=0, concat_axis=0, tiled=True)  50.2 us
    scatter-add x1, other arithmetic, local(): jax.ops.segment_sum(returned.reshape(-1, emb_width).astype(jnp.float32),...  40.9 us
    gather x1, local copies, waits for them, and re-layouts, local(): jnp.take(row_table, positions, axis=0).reshape(feat_count, -1, emb_width)  33 us
    reduce_sum x1, other arithmetic, summed_here(): result = parts.sum(axis=0)  14.3 us
  transfers between devices with their start and end apart: 3, of which 3 were waited for; matrix products, arithmetic and copies ran while one was open for 2% of the time, Pallas kernels for 0%

profile of v1, /device:TPU:1, one launch (start us, length us, event | category | flops | bytes accessed | tf_op | source)
XLA Modules:
  0.0 679.3 jit_solution(8447596960640439455)
XLA Ops:
  7.2 0.0 copy-start
  7.2 0.9 compare_select_fusion
  8.1 0.5 broadcast.66
  8.7 1.5 reduce.4
  10.2 0.0 copy-start.5
  10.2 9.8 %multiply_convert_fusion.2 = (bf16[768,2048]{1,0:T(8,128)(2,1)S(1)}, f32[768,2048]{1,0:T(8,128)}) fusion(bf16[1,1024,2048]{2,1,0:T(8,128)(2,1)} %param.10, s32[1,768,1024]{2,1,0:T(8,128)} %param.7), kind=kOutput, calls=%fused_computation.6 | convolution fusion | flops 3232235520 | bytes 16777216 | tf_op jit(solution)/shard_map/dot_general | solution.py:50
  20.0 0.0 copy-start.7
  20.0 1.6 copy-done.7
  21.7 0.0 copy-done.5
  21.7 1.0 convolution_convert_fusion.2
  22.7 33.0 %gather_fusion = bf16[8192,256]{1,0:T(8,128)(2,1)} fusion(bf16[768,256]{1,0:T(8,128)(2,1)S(1)} %convolution_convert_fusion.2, s32[8192]{0:T(1024)S(1)} %broadcast_clamp_fusion), kind=kCustom, calls=%fused_computation | custom fusion | bytes 8421376 | tf_op jit(solution)/shard_map/jit(_take)/gather | solution.py:58
  55.6 5.2 broadcast_select_fusion
  60.9 0.0 copy-start.3
  60.9 0.0 copy-start.4
  60.9 8.8 %all-to-all-start = ((bf16[32,256,256]{2,1,0:T(8,128)(2,1)}), bf16[32,256,256]{2,1,0:T(8,128)(2,1)}, u32[]{:S(2)}, u32[]{:S(2)}) async-start(bf16[32,256,256]{2,1,0:T(8,128)(2,1)} %broadcast_select_fusion), calls=%async_computation | async-start | bytes 8388608 | tf_op jit(solution)/shard_map/all_to_all | solution.py:59
  69.7 0.0 all-reduce.2.cloned.1.call-start
  69.7 0.0 copy-done.3
  69.7 0.0 copy-done.4
  69.8 50.2 %all-to-all-done = bf16[32,256,256]{2,1,0:T(8,128)(2,1)} async-done(((bf16[32,256,256]{2,1,0:T(8,128)(2,1)}), bf16[32,256,256]{2,1,0:T(8,128)(2,1)}, u32[]{:S(2)}, u32[]{:S(2)}) %all-to-all-start) | async-done | bytes 4194336 | tf_op jit(solution)/shard_map/all_to_all | solution.py:59
  119.9 10.2 %fusion.5 = f32[256,32,32]{2,1,0:T(8,128)} fusion(bf16[32,256,256]{2,1,0:T(8,128)(2,1)} %all-to-all-done), kind=kOutput, calls=%fused_computation.13 | convolution fusion | flops 134217728 | bytes 5242880 | tf_op jit(solution)/shard_map/fne,hne->nfh/dot_general | solution.py:24
  130.1 3.5 copy.33
  133.6 0.1 multiply_convert_fusion.5
  133.8 0.0 copy-done
  133.8 0.7 fusion.35
  134.5 0.4 fusion.20
  134.9 1.0 fusion.16
  135.9 0.6 fusion.12
  136.5 3.0 copy.37
  139.5 4.9 fusion.2
  144.5 2.4 copy.38
  146.9 57.9 %all_to_all.10 = bf16[32,256,256]{2,1,0:T(8,128)(2,1)} all-to-all(bf16[32,256,256]{2,1,0:T(8,128)(2,1)S(1)} %copy.38), channel_id=1, replica_groups=mesh['feat'=32,'samp'=8] {'feat'}, dimensions={0} | all-to-all | bytes 8388608 | tf_op jit(solution)/shard_map/all_to_all | solution.py:61
  204.8 40.9 %scatter_custom_fusion = f32[768,256]{1,0:T(8,128)S(1)} fusion(s32[8192]{0:T(1024)} %bitcast.53, bf16[8192,256]{1,0:T(8,128)(2,1)} %bitcast.48, f32[]{:T(128)} %constant.16.clone.1), kind=kCustom, calls=%fused_computation.2 | custom fusion | flops 4194304 | bytes 4981248 | tf_op jit(solution)/shard_map/scatter-add | solution.py:62
  245.7 0.0 copy-start.2
  245.7 0.0 copy-start.6
  245.7 4.2 convolution_convert_fusion.1
  249.9 0.0 all-reduce.2.cloned.1.call-update
  250.0 0.0 all-gather.3.cloned.1.call-start
  250.0 0.0 copy-done.2
  250.0 0.0 copy-done.6
  250.0 10.2 %convolution_convert_fusion = bf16[1024,2048]{1,0:T(8,128)(2,1)} fusion(f32[768,2048]{1,0:T(8,128)} %get-tuple-element.4, bf16[1,2048,256]{2,1,0:T(8,128)(2,1)S(1)} %copy-done.6, s32[1,768,1024]{2,1,0:T(8,128)} %param.7, f32[768,256]{1,0:T(8,128)S(1)} %scatter_custom_fusion), kind=kOutput, calls=%fused_computation.12 | convolution fusion | flops 4046127104 | bytes 15466496 | tf_op jit(solution)/shard_map/rh,rk->hk/dot_general | solution.py:73
  260.2 0.0 all-gather.3.cloned.1.call-update
  260.2 61.5 %all-reduce.2.cloned.1.call-done = bf16[2048,256]{1,0:T(8,128)(2,1)} async-done(((bf16[2048,256]{1,0:T(8,128)(2,1)}), bf16[2048,256]{1,0:T(8,128)(2,1)}) %all-reduce.2.cloned.1.call-update) | async-done | bytes 1048592 | tf_op jit(solution)/shard_map/psum | solution.py:76
  321.7 1.6 convert_bitcast_fusion.1
  323.3 332.7 %all-gather.3.cloned.1.call-done = bf16[8192,2048]{1,0:T(8,128)(2,1)} async-done(((bf16[1024,2048]{1,0:T(8,128)(2,1)}), bf16[8192,2048]{1,0:T(8,128)(2,1)}) %all-gather.3.cloned.1.call-update) | async-done | bytes 33554448 | tf_op jit(solution)/shard_map/all_gather | solution.py:11
  656.0 0.0 copy-start.1
  656.0 14.3 %reduce_sum.12 = bf16[1024,2048]{1,0:T(8,128)(2,1)} reduce(bf16[8,1024,2048]{2,1,0:T(8,128)(2,1)} %bitcast.47, bf16[]{:T(256)} %constant.13.clone.1), dimensions={0}, to_apply=%region_1.2 | reduce | flops 14680064 | bytes 37748736 | tf_op jit(solution)/shard_map/reduce_sum | solution.py:12
  670.3 2.1 convert_bitcast_fusion
  672.4 0.0 copy-done.1
  (7 shorter events, 0.1 us)
Async XLA Ops:
  7.2 126.6 %copy-start = (bf16[1024,1024]{1,0:T(8,128)(2,1)S(1)}, bf16[1024,1024]{1,0:T(8,128)(2,1)}, u32[]{:S(2)}) copy-start(bf16[1024,1024]{1,0:T(8,128)(2,1)} %param.12) | copy-start | bytes 6291460
  10.2 11.5 %copy-start.5 = (bf16[1,2048,256]{2,1,0:T(8,128)(2,1)S(1)}, bf16[1,2048,256]{2,1,0:T(8,128)(2,1)}, u32[]{:S(2)}) copy-start(bf16[1,2048,256]{2,1,0:T(8,128)(2,1)} %param.11) | copy-start | bytes 3145732
  20.0 1.6 copy-start.7
  60.9 8.8 %copy-start.3 = (bf16[1024]{0:T(1024)(128)(2,1)S(1)}, bf16[1024]{0:T(1024)(128)(2,1)}, u32[]{:S(2)}) copy-start(bf16[1024]{0:T(1024)(128)(2,1)} %param.13) | copy-start | bytes 6148
  60.9 8.9 %copy-start.4 = (s32[256,1]{0,1:T(1,128)S(1)}, s32[256,1]{0,1:T(1,128)}, u32[]{:S(2)}) copy-start(s32[256,1]{0,1:T(1,128)} %param.9) | copy-start | bytes 3076
  60.9 59.0 %all-to-all-start = ((bf16[32,256,256]{2,1,0:T(8,128)(2,1)}), bf16[32,256,256]{2,1,0:T(8,128)(2,1)}, u32[]{:S(2)}, u32[]{:S(2)}) async-start(bf16[32,256,256]{2,1,0:T(8,128)(2,1)} %broadcast_select_fusion), calls=%async_computation | async-start | bytes 8388608 | tf_op jit(solution)/shard_map/all_to_all | solution.py:59
  69.7 252.0 %all-reduce.2.cloned.1.call-start = ((), (), s32[]{:S(2)}) async-start(), calls=%async_computation.2 | async-start | bytes 2097152 | tf_op jit(solution)/shard_map/psum | solution.py:76
  245.7 4.3 copy-start.2
  245.7 4.3 copy-start.6
  250.0 406.0 %all-gather.3.cloned.1.call-start = ((), (), s32[]{:S(2)}) async-start(), calls=%async_computation.3 | async-start | bytes 37748736 | tf_op jit(solution)/shard_map/all_gather | solution.py:11
  656.0 16.4 %copy-start.1 = (bf16[1024,1024]{1,0:T(8,128)(2,1)S(1)}, bf16[1024,1024]{1,0:T(8,128)(2,1)}, u32[]{:S(2)}) copy-start(bf16[1024,1024]{1,0:T(8,128)(2,1)} %param.12) | copy-start | bytes 6291460
Sparse Core Ops, SparseCore 0:
  250.1 71.5 all-reduce.1
  323.5 332.4 all-gather.2
